TPU v7x, 512 devices: a whole 4x8x8 slice. The times are simulated.
512 devices in a mesh: tm: 16 (over z, y_hi), space: 32 (over x, y_lo, core).
Axes of the slice: x: 4, y: 8 (y_hi: 2, y_lo: 4; y = y_hi * 4 + y_lo), z: 8, core: 2. Of those that a mesh axis runs over, the one named last changes fastest.
Arguments:
- state: float32 [16, 5, 256, 32, 128], P('tm', None, 'space'), may hold values from -6 to 6
- base: float32 [16, 5, 256, 32, 128], P('tm', None, 'space'), may hold values from -6 to 6
- pseudo_step: float32 [256, 32, 128], P('space'), may hold values from 0.05 to 0.3
- eddy_visc: float32 [256, 32, 128], P('space'), may hold values from 0.02 to 0.2
- jacobians: float32 [3, 5, 5], replicated, may hold values from -2.5 to 2.5
- partner_radial: int32 [2, 256, 128], P(None, 'space'), may hold values from 0 to 127, each once within a row
- partner_instance: int32 [16, 2, 256, 128], P('tm', None, 'space'), may hold values from 0 to 15, as said below
Outputs:
- updated: float32 [16, 5, 256, 32, 128], P('tm', None, 'space')
Inputs may be any that keep to these rules, and one draw needn't show every extreme that they name: partner_radial[s, i, :] is a permutation of the radial indices 0..127: the partner cells on the opposite periodic face in the same axial plane. partner_instance[n, 0, i, k] = (n + L_i) mod 16 and partner_instance[n, 1, i, k] = (n - L_i) mod 16 for a lag L_i in 1..15 that depends only on the axial plane i.
All inputs are finite; a program needn't handle non-finite values.
Results may differ from a plain program's by a relative error of at most 0.00005.
Values sent between devices are 32-bit elements; how exact they have to be, the bound alone decides.
No kernel may reach another device: no remote copies, remote signals or barrier semaphores. Data moves between devices by JAX's collectives and lax.ppermute only.
A program may use at most 64 MiB of HBM per device.

v0:
```python
import math
import jax
import jax.numpy as jnp
from jax import lax
from jax.sharding import PartitionSpec as P

SECTION_ALPHA = 0.5
PITCH_ANGLE = 2.0 * math.pi / 36.0
NYQUIST_DAMP = 2.0


def shifted(value, axis, by):
    devices = lax.axis_size(axis)
    return lax.ppermute(value, axis, [(i, (i + by) % devices) for i in range(devices)])


def extended_2(block, sides, width):
    for axis, dim in sides:
        count = lax.axis_size(axis)
        forward = [(i, i + 1) for i in range(count - 1)]
        backward = [(target, source) for source, target in forward]
        low = lax.ppermute(
            lax.slice_in_dim(block, block.shape[dim] - width, None, axis=dim), axis, forward
        )
        high = lax.ppermute(lax.slice_in_dim(block, 0, width, axis=dim), axis, backward)
        block = jnp.concatenate([low, block, high], axis=dim)
    return block


def time_weights(offset, count):
    offset = offset % count
    angle = math.pi * offset.astype(jnp.float32) / count
    parity = jnp.where(offset % 2 == 1, 1.0, -1.0).astype(jnp.float32)
    sine = jnp.where(offset == 0, 1.0, jnp.sin(angle))
    spectral = 0.5 * parity * jnp.cos(angle) / sine - NYQUIST_DAMP * parity / count
    return jnp.where(offset == 0, NYQUIST_DAMP / count, spectral)


def rotate_velocity(values, turn):
    cosine = math.cos(PITCH_ANGLE)
    sine = turn * math.sin(PITCH_ANGLE)
    second = values[:, 2]
    third = values[:, 3]
    return jnp.stack(
        [
            values[:, 0],
            values[:, 1],
            cosine * second - sine * third,
            sine * second + cosine * third,
            values[:, 4],
        ],
        axis=1,
    )


def section_update(
    state, base, pseudo_step, eddy_visc, jacobians, up_i, down_i, low_ghost, high_ghost, time_term
):
    up_j = jnp.concatenate([state[:, :, :, 1:], high_ghost[:, :, :, None]], axis=3)
    down_j = jnp.concatenate([low_ghost[:, :, :, None], state[:, :, :, :-1]], axis=3)
    zeros = jnp.zeros(state.shape[:4] + (1,), state.dtype)
    up_k = jnp.concatenate([state[..., 1:], zeros], axis=4)
    down_k = jnp.concatenate([zeros, state[..., :-1]], axis=4)
    diffs = jnp.stack([up_i - down_i, up_j - down_j, up_k - down_k], axis=0) * 0.5
    flux = jnp.einsum("dab,dnbijk->naijk", jacobians, diffs, precision=lax.Precision.HIGHEST)
    laplace = up_i + down_i + up_j + down_j + up_k + down_k - 6.0 * state
    spatial = flux - eddy_visc[None, None] * laplace
    return base - SECTION_ALPHA * pseudo_step[None, None] * (spatial + time_term)


def radial_table(partner_radial):
    radial_count = partner_radial.shape[2]
    radial_ids = jnp.arange(radial_count, dtype=jnp.int32)
    return (partner_radial[..., None] == radial_ids).astype(jnp.float32)


def per_device(state, base, pseudo_step, eddy_visc, jacobians, partner_radial, partner_instance):
    local_count = state.shape[0]
    cycle_size = lax.axis_size("tm")
    total_count = local_count * cycle_size
    position = lax.axis_index("tm")
    local_ids = jnp.arange(local_count, dtype=jnp.int32)
    own_ids = position * local_count + local_ids
    flattened = state.reshape(local_count, -1)
    start_weights = time_weights(own_ids[:, None] - own_ids[None, :], total_count)
    initial = jnp.dot(start_weights, flattened, precision=lax.Precision.HIGHEST)

    def one_turn(turn_index, carry):
        moving, accumulated = carry
        moving = shifted(moving, "tm", 1)
        anchor = (position - turn_index) % cycle_size
        source_ids = anchor * local_count + local_ids
        weights = time_weights(own_ids[:, None] - source_ids[None, :], total_count)
        return (moving, accumulated + jnp.dot(weights, moving, precision=lax.Precision.HIGHEST))

    moved_last, accumulated = lax.fori_loop(1, cycle_size, one_turn, (flattened, initial))
    time_term = accumulated.reshape(state.shape)
    radial_hot = radial_table(partner_radial)
    face_planes = jnp.stack([state[:, :, :, -1, :], state[:, :, :, 0, :]], axis=1)
    all_faces = lax.all_gather(face_planes, "tm", axis=0, tiled=True)
    instance_ids = jnp.arange(total_count, dtype=jnp.int32)
    instance_hot = (partner_instance[:, :, :, 0][..., None] == instance_ids).astype(jnp.float32)
    picked = jnp.einsum(
        "nsim,msvik->nsvik", instance_hot, all_faces, precision=lax.Precision.HIGHEST
    )
    remapped = jnp.einsum("nsvir,sikr->nsvik", picked, radial_hot, precision=lax.Precision.HIGHEST)
    low_ghost = rotate_velocity(remapped[:, 0], -1.0)
    high_ghost = rotate_velocity(remapped[:, 1], 1.0)
    extended = extended_2(state, (("space", 2),), 1)
    up_i = extended[:, :, 2:]
    down_i = extended[:, :, :-2]
    return section_update(
        state,
        base,
        pseudo_step,
        eddy_visc,
        jacobians,
        up_i,
        down_i,
        low_ghost,
        high_ghost,
        time_term,
    )


def solution(mesh):
    return jax.shard_map(
        per_device,
        mesh=mesh,
        in_specs=(
            P("tm", None, "space", None, None),
            P("tm", None, "space", None, None),
            P("space", None, None),
            P("space", None, None),
            P(),
            P(None, "space", None),
            P("tm", None, "space", None),
        ),
        out_specs=P("tm", None, "space", None, None),
        check_vma=False,
    )
```

profile of v0, /device:TPU:64, one launch (start us, length us, event | category | flops | bytes accessed | tf_op | source)
XLA Modules:
  0.0 639.7 jit_solution(3489502226336061569)
XLA Ops:
  0.0 2.0 copy.106
  7.9 75.3 %all_gather.3 = f32[16,2,5,8,128]{4,3,2,1,0:T(8,128)S(1)} all-gather(f32[1,2,5,8,128]{4,3,2,1,0:T(8,128)S(1)} %pad_maximum_fusion.4), channel_id=1, replica_groups=mesh['tm'=16,'space'=32] {'tm'}, dimensions={0}, use_global_device_ids=true | all-gather | bytes 696320 | tf_op jit(solution)/shard_map/all_gather | solution.py:100
  89.6 2.7 pad_subtract_fusion
  94.7 536.5 %while.18 = (s32[]{:T(128)}, f32[1,163840]{1,0:T(1,128)}, f32[1,163840]{1,0:T(1,128)S(1)}, s32[]{:T(128)}, s32[]{:T(128)}, /*index=5*/s32[]{:T(128)}, s32[]{:T(1...) while((s32[]{:T(128)}, f32[1,163840]{1,0:T(1,128)}, ...), condition=%wide.region_1.2_spmd, body=%wide.region_0.1_spmd.sunk | while | flops 327729 | bytes 5898953 | solution.py:96
  96.8 21.0 %collective-permute-done = f32[1,163840]{1,0:T(1,128)S(1)} collective-permute-done((f32[1,163840]{1,0:T(1,128)}, f32[1,163840]{1,0:T(1,128)S(1)}, u32[]{:S(2)}, u32[]{:S(2)}) %collective-permute-start) | collective-permute-done | bytes 655392 | tf_op jit(solution)/shard_map/while/body/eval_jaxpr/ppermute | solution.py:14
  119.5 1.9 collective-permute-start
  121.6 25.5 %collective-permute-done = f32[1,163840]{1,0:T(1,128)S(1)} collective-permute-done((f32[1,163840]{1,0:T(1,128)}, f32[1,163840]{1,0:T(1,128)S(1)}, u32[]{:S(2)}, u32[]{:S(2)}) %collective-permute-start) | collective-permute-done | bytes 655392 | tf_op jit(solution)/shard_map/while/body/eval_jaxpr/ppermute | solution.py:14
  148.7 3.7 collective-permute-start
  152.6 24.9 %collective-permute-done = f32[1,163840]{1,0:T(1,128)S(1)} collective-permute-done((f32[1,163840]{1,0:T(1,128)}, f32[1,163840]{1,0:T(1,128)S(1)}, u32[]{:S(2)}, u32[]{:S(2)}) %collective-permute-start) | collective-permute-done | bytes 655392 | tf_op jit(solution)/shard_map/while/body/eval_jaxpr/ppermute | solution.py:14
  179.1 4.9 collective-permute-start
  184.2 19.7 %collective-permute-done = f32[1,163840]{1,0:T(1,128)S(1)} collective-permute-done((f32[1,163840]{1,0:T(1,128)}, f32[1,163840]{1,0:T(1,128)S(1)}, u32[]{:S(2)}, u32[]{:S(2)}) %collective-permute-start) | collective-permute-done | bytes 655392 | tf_op jit(solution)/shard_map/while/body/eval_jaxpr/ppermute | solution.py:14
  205.6 8.2 %collective-permute-start = (f32[1,163840]{1,0:T(1,128)}, f32[1,163840]{1,0:T(1,128)S(1)}, u32[]{:S(2)}, u32[]{:S(2)}) collective-permute-start(f32[1,163840]{1,0:T(1,128)} %get-tuple-element.213), channel_id=1, source_target_pairs={{0,32},{32,64},{64,96},{96,128},{128,160},{160,192},{192,224},{224... | collective-permute-start | bytes 1966088 | tf_op jit(solution)/shard_map/while/body/eval_jaxpr/ppermute | solution.py:14
  214.1 36.3 %collective-permute-done = f32[1,163840]{1,0:T(1,128)S(1)} collective-permute-done((f32[1,163840]{1,0:T(1,128)}, f32[1,163840]{1,0:T(1,128)S(1)}, u32[]{:S(2)}, u32[]{:S(2)}) %collective-permute-start) | collective-permute-done | bytes 655392 | tf_op jit(solution)/shard_map/while/body/eval_jaxpr/ppermute | solution.py:14
  251.9 1.9 collective-permute-start
  254.1 27.1 %collective-permute-done = f32[1,163840]{1,0:T(1,128)S(1)} collective-permute-done((f32[1,163840]{1,0:T(1,128)}, f32[1,163840]{1,0:T(1,128)S(1)}, u32[]{:S(2)}, u32[]{:S(2)}) %collective-permute-start) | collective-permute-done | bytes 655392 | tf_op jit(solution)/shard_map/while/body/eval_jaxpr/ppermute | solution.py:14
  282.8 8.3 %collective-permute-start = (f32[1,163840]{1,0:T(1,128)}, f32[1,163840]{1,0:T(1,128)S(1)}, u32[]{:S(2)}, u32[]{:S(2)}) collective-permute-start(f32[1,163840]{1,0:T(1,128)} %get-tuple-element.213), channel_id=1, source_target_pairs={{0,32},{32,64},{64,96},{96,128},{128,160},{160,192},{192,224},{224... | collective-permute-start | bytes 1966088 | tf_op jit(solution)/shard_map/while/body/eval_jaxpr/ppermute | solution.py:14
  291.4 42.6 %collective-permute-done = f32[1,163840]{1,0:T(1,128)S(1)} collective-permute-done((f32[1,163840]{1,0:T(1,128)}, f32[1,163840]{1,0:T(1,128)S(1)}, u32[]{:S(2)}, u32[]{:S(2)}) %collective-permute-start) | collective-permute-done | bytes 655392 | tf_op jit(solution)/shard_map/while/body/eval_jaxpr/ppermute | solution.py:14
  335.6 1.9 collective-permute-start
  337.8 37.0 %collective-permute-done = f32[1,163840]{1,0:T(1,128)S(1)} collective-permute-done((f32[1,163840]{1,0:T(1,128)}, f32[1,163840]{1,0:T(1,128)S(1)}, u32[]{:S(2)}, u32[]{:S(2)}) %collective-permute-start) | collective-permute-done | bytes 655392 | tf_op jit(solution)/shard_map/while/body/eval_jaxpr/ppermute | solution.py:14
  376.4 8.2 %collective-permute-start = (f32[1,163840]{1,0:T(1,128)}, f32[1,163840]{1,0:T(1,128)S(1)}, u32[]{:S(2)}, u32[]{:S(2)}) collective-permute-start(f32[1,163840]{1,0:T(1,128)} %get-tuple-element.213), channel_id=1, source_target_pairs={{0,32},{32,64},{64,96},{96,128},{128,160},{160,192},{192,224},{224... | collective-permute-start | bytes 1966088 | tf_op jit(solution)/shard_map/while/body/eval_jaxpr/ppermute | solution.py:14
  384.9 40.9 %collective-permute-done = f32[1,163840]{1,0:T(1,128)S(1)} collective-permute-done((f32[1,163840]{1,0:T(1,128)}, f32[1,163840]{1,0:T(1,128)S(1)}, u32[]{:S(2)}, u32[]{:S(2)}) %collective-permute-start) | collective-permute-done | bytes 655392 | tf_op jit(solution)/shard_map/while/body/eval_jaxpr/ppermute | solution.py:14
  427.5 1.9 collective-permute-start
  429.6 35.7 %collective-permute-done = f32[1,163840]{1,0:T(1,128)S(1)} collective-permute-done((f32[1,163840]{1,0:T(1,128)}, f32[1,163840]{1,0:T(1,128)S(1)}, u32[]{:S(2)}, u32[]{:S(2)}) %collective-permute-start) | collective-permute-done | bytes 655392 | tf_op jit(solution)/shard_map/while/body/eval_jaxpr/ppermute | solution.py:14
  467.0 1.9 collective-permute-start
  469.1 25.5 %collective-permute-done = f32[1,163840]{1,0:T(1,128)S(1)} collective-permute-done((f32[1,163840]{1,0:T(1,128)}, f32[1,163840]{1,0:T(1,128)S(1)}, u32[]{:S(2)}, u32[]{:S(2)}) %collective-permute-start) | collective-permute-done | bytes 655392 | tf_op jit(solution)/shard_map/while/body/eval_jaxpr/ppermute | solution.py:14
  496.2 1.9 collective-permute-start
  498.4 36.0 %collective-permute-done = f32[1,163840]{1,0:T(1,128)S(1)} collective-permute-done((f32[1,163840]{1,0:T(1,128)}, f32[1,163840]{1,0:T(1,128)S(1)}, u32[]{:S(2)}, u32[]{:S(2)}) %collective-permute-start) | collective-permute-done | bytes 655392 | tf_op jit(solution)/shard_map/while/body/eval_jaxpr/ppermute | solution.py:14
  536.0 1.9 collective-permute-start
  538.2 28.6 %collective-permute-done = f32[1,163840]{1,0:T(1,128)S(1)} collective-permute-done((f32[1,163840]{1,0:T(1,128)}, f32[1,163840]{1,0:T(1,128)S(1)}, u32[]{:S(2)}, u32[]{:S(2)}) %collective-permute-start) | collective-permute-done | bytes 655392 | tf_op jit(solution)/shard_map/while/body/eval_jaxpr/ppermute | solution.py:14
  570.5 35.1 %collective-permute-done = f32[1,163840]{1,0:T(1,128)S(1)} collective-permute-done((f32[1,163840]{1,0:T(1,128)}, f32[1,163840]{1,0:T(1,128)S(1)}, u32[]{:S(2)}, u32[]{:S(2)}) %collective-permute-start) | collective-permute-done | bytes 655392 | tf_op jit(solution)/shard_map/while/body/eval_jaxpr/ppermute | solution.py:14
  609.4 20.2 %collective-permute-done = f32[1,163840]{1,0:T(1,128)S(1)} collective-permute-done((f32[1,163840]{1,0:T(1,128)}, f32[1,163840]{1,0:T(1,128)S(1)}, u32[]{:S(2)}, u32[]{:S(2)}) %collective-permute-start) | collective-permute-done | bytes 655392 | tf_op jit(solution)/shard_map/while/body/eval_jaxpr/ppermute | solution.py:14
  631.2 7.5 %fusion.10 = f32[1,5,8,32,128]{4,1,0,3,2:T(8,128)S(1)} fusion(f32[1,5,8,32,128]{4,1,0,3,2:T(8,128)} %pad_subtract_fusion, f32[1,5,8,32,128]{4,1,0,3,2:T(8,128)} %fusion.12, f32[1,5,8,32,128]{4,1,0,3,2:T(8,128)} %fusion.13, f32[1,5,8,32,128]{4,3,2,1,0:T(8,128)} %param.10, f32[1,5,8,32,128]{4,3,2,1,0:T(8,128)S(1)} %bitcast.55, ...), kind=kOutput, calls=%fused_computation.12 | convolution fusion | flops 33587200 | bytes 7625004 | tf_op jit(solution)/shard_map/dab,dnbijk->naijk/dot_general | solution.py:65
  (79 shorter events, 44.9 us)
Async XLA Ops:
  0.0 631.2 %copy-start = (f32[3,5,5]{2,0,1:T(4,128)S(1)}, f32[3,5,5]{2,0,1:T(4,128)}, u32[]{:S(2)}) copy-start(f32[3,5,5]{2,0,1:T(4,128)} %param.13) | copy-start | bytes 904
  2.0 5.6 copy-start.7
  3.5 80.2 %copy-start.8 = (s32[2,8,128]{2,1,0:T(8,128)S(1)}, s32[2,8,128]{2,1,0:T(8,128)}, u32[]{:S(2)}) copy-start(s32[2,8,128]{2,1,0:T(8,128)} %param.14) | copy-start | bytes 24580
  3.5 90.0 %collective-permute-start.2 = (f32[1,5,1,32,128]{4,1,0,3,2:T(8,128)S(1)}, f32[1,5,1,32,128]{4,1,0,3,2:T(8,128)S(1)}, u32[]{:S(2)}, u32[]{:S(2)}) collective-permute-start(f32[1,5,1,32,128]{4,1,0,3,2:T(8,128)S(1)} %get-tuple-element.150), channel_id=1, source_target_pairs={{0,1},{1,2},{2,3},{3,4},{4,5},{5,6},{6,7},{7,8},{8,9},{9,10},{10,1... | collective-permute-start | bytes 245768 | tf_op jit(solution)/shard_map/ppermute | solution.py:22
  5.3 88.2 %collective-permute-start.1 = (f32[1,5,1,32,128]{4,1,0,3,2:T(8,128)S(1)}, f32[1,5,1,32,128]{4,1,0,3,2:T(8,128)S(1)}, u32[]{:S(2)}, u32[]{:S(2)}) collective-permute-start(f32[1,5,1,32,128]{4,1,0,3,2:T(8,128)S(1)} %get-tuple-element.151), channel_id=1, source_target_pairs={{1,0},{2,1},{3,2},{4,3},{5,4},{6,5},{7,6},{8,7},{9,8},{10,9},{11,1... | collective-permute-start | bytes 245768 | tf_op jit(solution)/shard_map/ppermute | solution.py:25
  87.6 1.3 copy-start.6
  89.6 2.8 copy-start.4
  89.6 2.7 copy-start.5
  89.6 2.7 copy-start.1
  89.6 2.7 copy-start.2
  93.5 1.1 copy-start.3
  94.7 23.2 %collective-permute-start = (f32[1,163840]{1,0:T(1,128)}, f32[1,163840]{1,0:T(1,128)S(1)}, u32[]{:S(2)}, u32[]{:S(2)}) collective-permute-start(f32[1,163840]{1,0:T(1,128)} %get-tuple-element.213), channel_id=1, source_target_pairs={{0,32},{32,64},{64,96},{96,128},{128,160},{160,192},{192,224},{224... | collective-permute-start | bytes 1966088 | tf_op jit(solution)/shard_map/while/body/eval_jaxpr/ppermute | solution.py:14
  119.5 27.7 %collective-permute-start = (f32[1,163840]{1,0:T(1,128)}, f32[1,163840]{1,0:T(1,128)S(1)}, u32[]{:S(2)}, u32[]{:S(2)}) collective-permute-start(f32[1,163840]{1,0:T(1,128)} %get-tuple-element.213), channel_id=1, source_target_pairs={{0,32},{32,64},{64,96},{96,128},{128,160},{160,192},{192,224},{224... | collective-permute-start | bytes 1966088 | tf_op jit(solution)/shard_map/while/body/eval_jaxpr/ppermute | solution.py:14
  148.7 28.8 %collective-permute-start = (f32[1,163840]{1,0:T(1,128)}, f32[1,163840]{1,0:T(1,128)S(1)}, u32[]{:S(2)}, u32[]{:S(2)}) collective-permute-start(f32[1,163840]{1,0:T(1,128)} %get-tuple-element.213), channel_id=1, source_target_pairs={{0,32},{32,64},{64,96},{96,128},{128,160},{160,192},{192,224},{224... | collective-permute-start | bytes 1966088 | tf_op jit(solution)/shard_map/while/body/eval_jaxpr/ppermute | solution.py:14
  179.1 24.9 %collective-permute-start = (f32[1,163840]{1,0:T(1,128)}, f32[1,163840]{1,0:T(1,128)S(1)}, u32[]{:S(2)}, u32[]{:S(2)}) collective-permute-start(f32[1,163840]{1,0:T(1,128)} %get-tuple-element.213), channel_id=1, source_target_pairs={{0,32},{32,64},{64,96},{96,128},{128,160},{160,192},{192,224},{224... | collective-permute-start | bytes 1966088 | tf_op jit(solution)/shard_map/while/body/eval_jaxpr/ppermute | solution.py:14
  205.6 44.8 %collective-permute-start = (f32[1,163840]{1,0:T(1,128)}, f32[1,163840]{1,0:T(1,128)S(1)}, u32[]{:S(2)}, u32[]{:S(2)}) collective-permute-start(f32[1,163840]{1,0:T(1,128)} %get-tuple-element.213), channel_id=1, source_target_pairs={{0,32},{32,64},{64,96},{96,128},{128,160},{160,192},{192,224},{224... | collective-permute-start | bytes 1966088 | tf_op jit(solution)/shard_map/while/body/eval_jaxpr/ppermute | solution.py:14
  251.9 29.3 %collective-permute-start = (f32[1,163840]{1,0:T(1,128)}, f32[1,163840]{1,0:T(1,128)S(1)}, u32[]{:S(2)}, u32[]{:S(2)}) collective-permute-start(f32[1,163840]{1,0:T(1,128)} %get-tuple-element.213), channel_id=1, source_target_pairs={{0,32},{32,64},{64,96},{96,128},{128,160},{160,192},{192,224},{224... | collective-permute-start | bytes 1966088 | tf_op jit(solution)/shard_map/while/body/eval_jaxpr/ppermute | solution.py:14
  282.8 51.2 %collective-permute-start = (f32[1,163840]{1,0:T(1,128)}, f32[1,163840]{1,0:T(1,128)S(1)}, u32[]{:S(2)}, u32[]{:S(2)}) collective-permute-start(f32[1,163840]{1,0:T(1,128)} %get-tuple-element.213), channel_id=1, source_target_pairs={{0,32},{32,64},{64,96},{96,128},{128,160},{160,192},{192,224},{224... | collective-permute-start | bytes 1966088 | tf_op jit(solution)/shard_map/while/body/eval_jaxpr/ppermute | solution.py:14
  335.6 39.2 %collective-permute-start = (f32[1,163840]{1,0:T(1,128)}, f32[1,163840]{1,0:T(1,128)S(1)}, u32[]{:S(2)}, u32[]{:S(2)}) collective-permute-start(f32[1,163840]{1,0:T(1,128)} %get-tuple-element.213), channel_id=1, source_target_pairs={{0,32},{32,64},{64,96},{96,128},{128,160},{160,192},{192,224},{224... | collective-permute-start | bytes 1966088 | tf_op jit(solution)/shard_map/while/body/eval_jaxpr/ppermute | solution.py:14
  376.4 49.4 %collective-permute-start = (f32[1,163840]{1,0:T(1,128)}, f32[1,163840]{1,0:T(1,128)S(1)}, u32[]{:S(2)}, u32[]{:S(2)}) collective-permute-start(f32[1,163840]{1,0:T(1,128)} %get-tuple-element.213), channel_id=1, source_target_pairs={{0,32},{32,64},{64,96},{96,128},{128,160},{160,192},{192,224},{224... | collective-permute-start | bytes 1966088 | tf_op jit(solution)/shard_map/while/body/eval_jaxpr/ppermute | solution.py:14
  427.5 37.9 %collective-permute-start = (f32[1,163840]{1,0:T(1,128)}, f32[1,163840]{1,0:T(1,128)S(1)}, u32[]{:S(2)}, u32[]{:S(2)}) collective-permute-start(f32[1,163840]{1,0:T(1,128)} %get-tuple-element.213), channel_id=1, source_target_pairs={{0,32},{32,64},{64,96},{96,128},{128,160},{160,192},{192,224},{224... | collective-permute-start | bytes 1966088 | tf_op jit(solution)/shard_map/while/body/eval_jaxpr/ppermute | solution.py:14
  467.0 27.6 %collective-permute-start = (f32[1,163840]{1,0:T(1,128)}, f32[1,163840]{1,0:T(1,128)S(1)}, u32[]{:S(2)}, u32[]{:S(2)}) collective-permute-start(f32[1,163840]{1,0:T(1,128)} %get-tuple-element.213), channel_id=1, source_target_pairs={{0,32},{32,64},{64,96},{96,128},{128,160},{160,192},{192,224},{224... | collective-permute-start | bytes 1966088 | tf_op jit(solution)/shard_map/while/body/eval_jaxpr/ppermute | solution.py:14
  496.2 38.2 %collective-permute-start = (f32[1,163840]{1,0:T(1,128)}, f32[1,163840]{1,0:T(1,128)S(1)}, u32[]{:S(2)}, u32[]{:S(2)}) collective-permute-start(f32[1,163840]{1,0:T(1,128)} %get-tuple-element.213), channel_id=1, source_target_pairs={{0,32},{32,64},{64,96},{96,128},{128,160},{160,192},{192,224},{224... | collective-permute-start | bytes 1966088 | tf_op jit(solution)/shard_map/while/body/eval_jaxpr/ppermute | solution.py:14
  536.0 30.7 %collective-permute-start = (f32[1,163840]{1,0:T(1,128)}, f32[1,163840]{1,0:T(1,128)S(1)}, u32[]{:S(2)}, u32[]{:S(2)}) collective-permute-start(f32[1,163840]{1,0:T(1,128)} %get-tuple-element.213), channel_id=1, source_target_pairs={{0,32},{32,64},{64,96},{96,128},{128,160},{160,192},{192,224},{224... | collective-permute-start | bytes 1966088 | tf_op jit(solution)/shard_map/while/body/eval_jaxpr/ppermute | solution.py:14
  568.4 37.2 %collective-permute-start = (f32[1,163840]{1,0:T(1,128)}, f32[1,163840]{1,0:T(1,128)S(1)}, u32[]{:S(2)}, u32[]{:S(2)}) collective-permute-start(f32[1,163840]{1,0:T(1,128)} %get-tuple-element.213), channel_id=1, source_target_pairs={{0,32},{32,64},{64,96},{96,128},{128,160},{160,192},{192,224},{224... | collective-permute-start | bytes 1966088 | tf_op jit(solution)/shard_map/while/body/eval_jaxpr/ppermute | solution.py:14
  607.2 22.4 %collective-permute-start = (f32[1,163840]{1,0:T(1,128)}, f32[1,163840]{1,0:T(1,128)S(1)}, u32[]{:S(2)}, u32[]{:S(2)}) collective-permute-start(f32[1,163840]{1,0:T(1,128)} %get-tuple-element.213), channel_id=1, source_target_pairs={{0,32},{32,64},{64,96},{96,128},{128,160},{160,192},{192,224},{224... | collective-permute-start | bytes 1966088 | tf_op jit(solution)/shard_map/while/body/eval_jaxpr/ppermute | solution.py:14
where the time goes:
time: 640 us
  waiting for transfers between devices  456 us (71%)
  blocking collectives  75.3 us (12%)
  starting transfers between devices  55.5 us (9%)
  local copies, waits for them, and re-layouts  21 us (3%)
  other arithmetic  18.1 us (3%)
  matrix products  9.23 us (1%)
    ppermute x15, waiting for transfers between devices, shifted(): lax.ppermute(value, axis, [(i, (i + by) % devices) for i in range(devices)])  456 us
    all_gather x1, blocking collectives, per_device(): all_faces = lax.all_gather(face_planes, 'tm', axis=0, tiled=True)  75.3 us
    ppermute x15, starting transfers between devices, shifted(): lax.ppermute(value, axis, [(i, (i + by) % devices) for i in range(devices)])  52.5 us
  transfers between devices with their start and end apart: 17, of which 15 were waited for; matrix products, arithmetic and copies ran while one was open for 2% of the time, Pallas kernels for 0%

commit v1 on v0

--- a/solution.py
+++ b/solution.py
@@ -97,7 +97,9 @@
     time_term = accumulated.reshape(state.shape)
     radial_hot = radial_table(partner_radial)
     face_planes = jnp.stack([state[:, :, :, -1, :], state[:, :, :, 0, :]], axis=1)
-    all_faces = lax.all_gather(face_planes, "tm", axis=0, tiled=True)
+    all_faces = jnp.concatenate(
+        lax.all_to_all(jnp.stack([face_planes] * lax.axis_size("tm")), "tm", 0, 0), axis=0
+    )
     instance_ids = jnp.arange(total_count, dtype=jnp.int32)
     instance_hot = (partner_instance[:, :, :, 0][..., None] == instance_ids).astype(jnp.float32)
     picked = jnp.einsum(

time: 640 us -> 603 us (0.942)
  the two profiles are of different devices: /device:TPU:64 before, /device:TPU:184 now
where the time goes in v1:
time: 603 us; the launch traced here: 602 us
  waiting for transfers between devices  384 us (64%)
  starting transfers between devices  167 us (28%)
  local copies, waits for them, and re-layouts  18.7 us (3%)
  other arithmetic  17.8 us (3%)
  matrix products  9.91 us (2%)
    ppermute x15, waiting for transfers between devices, shifted(): lax.ppermute(value, axis, [(i, (i + by) % devices) for i in range(devices)])  373 us
    ppermute x15, starting transfers between devices, shifted(): lax.ppermute(value, axis, [(i, (i + by) % devices) for i in range(devices)])  148 us
    all_to_all x1, starting transfers between devices, per_device(): lax.all_to_all(jnp.stack([face_planes] * lax.axis_size('tm')), 'tm', 0, 0)  13.9 us
    while x15, local copies, waits for them, and re-layouts  12.5 us
  transfers between devices with their start and end apart: 18, of which 17 were waited for; matrix products, arithmetic and copies ran while one was open for 1% of the time, Pallas kernels for 0%

profile of v1, /device:TPU:184, one launch (start us, length us, event | category | flops | bytes accessed | tf_op | source)
XLA Modules:
  0.0 602.2 jit_solution(88207624544019652)
XLA Ops:
  2.1 13.9 %all-to-all-start = ((f32[16,1,2,5,8,128]{5,4,3,2,1,0:T(8,128)}), f32[16,1,2,5,8,128]{5,4,3,2,1,0:T(8,128)S(1)}, u32[]{:S(2)}, u32[]{:S(2)}) async-start(f32[16,1,2,5,8,128]{5,4,3,2,1,0:T(8,128)} %stack.16), calls=%async_computation | async-start | bytes 1310720 | tf_op jit(solution)/shard_map/all_to_all | solution.py:101
  19.1 3.6 collective-permute-start.1
  26.9 6.1 %collective-permute-done.2 = f32[1,5,1,32,128]{4,1,0,3,2:T(8,128)S(1)} collective-permute-done((f32[1,5,1,32,128]{4,1,0,3,2:T(8,128)}, f32[1,5,1,32,128]{4,1,0,3,2:T(8,128)S(1)}, u32[]{:S(2)}, u32[]{:S(2)}) %collective-permute-start.2) | collective-permute-done | bytes 81952 | tf_op jit(solution)/shard_map/ppermute | solution.py:22
  33.0 4.7 collective-permute-done.1
  44.7 549.0 %while.18 = (s32[]{:T(128)}, f32[1,163840]{1,0:T(1,128)}, f32[1,163840]{1,0:T(1,128)S(1)}, s32[]{:T(128)}, s32[]{:T(128)}, /*index=5*/s32[]{:T(128)}, s32[]{:T(1...) while((s32[]{:T(128)}, f32[1,163840]{1,0:T(1,128)}, ...), condition=%wide.region_1.2_spmd, body=%wide.region_0.1_spmd.sunk | while | flops 327729 | bytes 5898953 | solution.py:96
  46.9 34.5 %collective-permute-done = f32[1,163840]{1,0:T(1,128)S(1)} collective-permute-done((f32[1,163840]{1,0:T(1,128)}, f32[1,163840]{1,0:T(1,128)S(1)}, u32[]{:S(2)}, u32[]{:S(2)}) %collective-permute-start) | collective-permute-done | bytes 655392 | tf_op jit(solution)/shard_map/while/body/eval_jaxpr/ppermute | solution.py:14
  85.1 16.0 %collective-permute-done = f32[1,163840]{1,0:T(1,128)S(1)} collective-permute-done((f32[1,163840]{1,0:T(1,128)}, f32[1,163840]{1,0:T(1,128)S(1)}, u32[]{:S(2)}, u32[]{:S(2)}) %collective-permute-start) | collective-permute-done | bytes 655392 | tf_op jit(solution)/shard_map/while/body/eval_jaxpr/ppermute | solution.py:14
  102.6 3.6 collective-permute-start
  106.5 21.6 %collective-permute-done = f32[1,163840]{1,0:T(1,128)S(1)} collective-permute-done((f32[1,163840]{1,0:T(1,128)}, f32[1,163840]{1,0:T(1,128)S(1)}, u32[]{:S(2)}, u32[]{:S(2)}) %collective-permute-start) | collective-permute-done | bytes 655392 | tf_op jit(solution)/shard_map/while/body/eval_jaxpr/ppermute | solution.py:14
  129.7 25.1 %collective-permute-start = (f32[1,163840]{1,0:T(1,128)}, f32[1,163840]{1,0:T(1,128)S(1)}, u32[]{:S(2)}, u32[]{:S(2)}) collective-permute-start(f32[1,163840]{1,0:T(1,128)} %get-tuple-element.213), channel_id=1, source_target_pairs={{0,32},{32,64},{64,96},{96,128},{128,160},{160,192},{192,224},{224... | collective-permute-start | bytes 1966088 | tf_op jit(solution)/shard_map/while/body/eval_jaxpr/ppermute | solution.py:14
  155.1 26.9 %collective-permute-done = f32[1,163840]{1,0:T(1,128)S(1)} collective-permute-done((f32[1,163840]{1,0:T(1,128)}, f32[1,163840]{1,0:T(1,128)S(1)}, u32[]{:S(2)}, u32[]{:S(2)}) %collective-permute-start) | collective-permute-done | bytes 655392 | tf_op jit(solution)/shard_map/while/body/eval_jaxpr/ppermute | solution.py:14
  183.6 25.5 %collective-permute-start = (f32[1,163840]{1,0:T(1,128)}, f32[1,163840]{1,0:T(1,128)S(1)}, u32[]{:S(2)}, u32[]{:S(2)}) collective-permute-start(f32[1,163840]{1,0:T(1,128)} %get-tuple-element.213), channel_id=1, source_target_pairs={{0,32},{32,64},{64,96},{96,128},{128,160},{160,192},{192,224},{224... | collective-permute-start | bytes 1966088 | tf_op jit(solution)/shard_map/while/body/eval_jaxpr/ppermute | solution.py:14
  209.3 27.2 %collective-permute-done = f32[1,163840]{1,0:T(1,128)S(1)} collective-permute-done((f32[1,163840]{1,0:T(1,128)}, f32[1,163840]{1,0:T(1,128)S(1)}, u32[]{:S(2)}, u32[]{:S(2)}) %collective-permute-start) | collective-permute-done | bytes 655392 | tf_op jit(solution)/shard_map/while/body/eval_jaxpr/ppermute | solution.py:14
  238.1 11.9 %collective-permute-start = (f32[1,163840]{1,0:T(1,128)}, f32[1,163840]{1,0:T(1,128)S(1)}, u32[]{:S(2)}, u32[]{:S(2)}) collective-permute-start(f32[1,163840]{1,0:T(1,128)} %get-tuple-element.213), channel_id=1, source_target_pairs={{0,32},{32,64},{64,96},{96,128},{128,160},{160,192},{192,224},{224... | collective-permute-start | bytes 1966088 | tf_op jit(solution)/shard_map/while/body/eval_jaxpr/ppermute | solution.py:14
  250.3 21.6 %collective-permute-done = f32[1,163840]{1,0:T(1,128)S(1)} collective-permute-done((f32[1,163840]{1,0:T(1,128)}, f32[1,163840]{1,0:T(1,128)S(1)}, u32[]{:S(2)}, u32[]{:S(2)}) %collective-permute-start) | collective-permute-done | bytes 655392 | tf_op jit(solution)/shard_map/while/body/eval_jaxpr/ppermute | solution.py:14
  273.5 29.1 %collective-permute-start = (f32[1,163840]{1,0:T(1,128)}, f32[1,163840]{1,0:T(1,128)S(1)}, u32[]{:S(2)}, u32[]{:S(2)}) collective-permute-start(f32[1,163840]{1,0:T(1,128)} %get-tuple-element.213), channel_id=1, source_target_pairs={{0,32},{32,64},{64,96},{96,128},{128,160},{160,192},{192,224},{224... | collective-permute-start | bytes 1966088 | tf_op jit(solution)/shard_map/while/body/eval_jaxpr/ppermute | solution.py:14
  302.9 31.5 %collective-permute-done = f32[1,163840]{1,0:T(1,128)S(1)} collective-permute-done((f32[1,163840]{1,0:T(1,128)}, f32[1,163840]{1,0:T(1,128)S(1)}, u32[]{:S(2)}, u32[]{:S(2)}) %collective-permute-start) | collective-permute-done | bytes 655392 | tf_op jit(solution)/shard_map/while/body/eval_jaxpr/ppermute | solution.py:14
  336.0 9.1 %collective-permute-start = (f32[1,163840]{1,0:T(1,128)}, f32[1,163840]{1,0:T(1,128)S(1)}, u32[]{:S(2)}, u32[]{:S(2)}) collective-permute-start(f32[1,163840]{1,0:T(1,128)} %get-tuple-element.213), channel_id=1, source_target_pairs={{0,32},{32,64},{64,96},{96,128},{128,160},{160,192},{192,224},{224... | collective-permute-start | bytes 1966088 | tf_op jit(solution)/shard_map/while/body/eval_jaxpr/ppermute | solution.py:14
  345.4 24.8 %collective-permute-done = f32[1,163840]{1,0:T(1,128)S(1)} collective-permute-done((f32[1,163840]{1,0:T(1,128)}, f32[1,163840]{1,0:T(1,128)S(1)}, u32[]{:S(2)}, u32[]{:S(2)}) %collective-permute-start) | collective-permute-done | bytes 655392 | tf_op jit(solution)/shard_map/while/body/eval_jaxpr/ppermute | solution.py:14
  371.8 8.3 %collective-permute-start = (f32[1,163840]{1,0:T(1,128)}, f32[1,163840]{1,0:T(1,128)S(1)}, u32[]{:S(2)}, u32[]{:S(2)}) collective-permute-start(f32[1,163840]{1,0:T(1,128)} %get-tuple-element.213), channel_id=1, source_target_pairs={{0,32},{32,64},{64,96},{96,128},{128,160},{160,192},{192,224},{224... | collective-permute-start | bytes 1966088 | tf_op jit(solution)/shard_map/while/body/eval_jaxpr/ppermute | solution.py:14
  380.4 23.0 %collective-permute-done = f32[1,163840]{1,0:T(1,128)S(1)} collective-permute-done((f32[1,163840]{1,0:T(1,128)}, f32[1,163840]{1,0:T(1,128)S(1)}, u32[]{:S(2)}, u32[]{:S(2)}) %collective-permute-start) | collective-permute-done | bytes 655392 | tf_op jit(solution)/shard_map/while/body/eval_jaxpr/ppermute | solution.py:14
  405.0 7.3 %collective-permute-start = (f32[1,163840]{1,0:T(1,128)}, f32[1,163840]{1,0:T(1,128)S(1)}, u32[]{:S(2)}, u32[]{:S(2)}) collective-permute-start(f32[1,163840]{1,0:T(1,128)} %get-tuple-element.213), channel_id=1, source_target_pairs={{0,32},{32,64},{64,96},{96,128},{128,160},{160,192},{192,224},{224... | collective-permute-start | bytes 1966088 | tf_op jit(solution)/shard_map/while/body/eval_jaxpr/ppermute | solution.py:14
  412.6 37.3 %collective-permute-done = f32[1,163840]{1,0:T(1,128)S(1)} collective-permute-done((f32[1,163840]{1,0:T(1,128)}, f32[1,163840]{1,0:T(1,128)S(1)}, u32[]{:S(2)}, u32[]{:S(2)}) %collective-permute-start) | collective-permute-done | bytes 655392 | tf_op jit(solution)/shard_map/while/body/eval_jaxpr/ppermute | solution.py:14
  453.8 29.5 %collective-permute-done = f32[1,163840]{1,0:T(1,128)S(1)} collective-permute-done((f32[1,163840]{1,0:T(1,128)}, f32[1,163840]{1,0:T(1,128)S(1)}, u32[]{:S(2)}, u32[]{:S(2)}) %collective-permute-start) | collective-permute-done | bytes 655392 | tf_op jit(solution)/shard_map/while/body/eval_jaxpr/ppermute | solution.py:14
  488.5 31.4 %collective-permute-done = f32[1,163840]{1,0:T(1,128)S(1)} collective-permute-done((f32[1,163840]{1,0:T(1,128)}, f32[1,163840]{1,0:T(1,128)S(1)}, u32[]{:S(2)}, u32[]{:S(2)}) %collective-permute-start) | collective-permute-done | bytes 655392 | tf_op jit(solution)/shard_map/while/body/eval_jaxpr/ppermute | solution.py:14
  521.5 5.1 collective-permute-start
  526.8 16.6 %collective-permute-done = f32[1,163840]{1,0:T(1,128)S(1)} collective-permute-done((f32[1,163840]{1,0:T(1,128)}, f32[1,163840]{1,0:T(1,128)S(1)}, u32[]{:S(2)}, u32[]{:S(2)}) %collective-permute-start) | collective-permute-done | bytes 655392 | tf_op jit(solution)/shard_map/while/body/eval_jaxpr/ppermute | solution.py:14
  545.0 7.2 %collective-permute-start = (f32[1,163840]{1,0:T(1,128)}, f32[1,163840]{1,0:T(1,128)S(1)}, u32[]{:S(2)}, u32[]{:S(2)}) collective-permute-start(f32[1,163840]{1,0:T(1,128)} %get-tuple-element.213), channel_id=1, source_target_pairs={{0,32},{32,64},{64,96},{96,128},{128,160},{160,192},{192,224},{224... | collective-permute-start | bytes 1966088 | tf_op jit(solution)/shard_map/while/body/eval_jaxpr/ppermute | solution.py:14
  552.5 15.7 %collective-permute-done = f32[1,163840]{1,0:T(1,128)S(1)} collective-permute-done((f32[1,163840]{1,0:T(1,128)}, f32[1,163840]{1,0:T(1,128)S(1)}, u32[]{:S(2)}, u32[]{:S(2)}) %collective-permute-start) | collective-permute-done | bytes 655392 | tf_op jit(solution)/shard_map/while/body/eval_jaxpr/ppermute | solution.py:14
  569.8 6.5 %collective-permute-start = (f32[1,163840]{1,0:T(1,128)}, f32[1,163840]{1,0:T(1,128)S(1)}, u32[]{:S(2)}, u32[]{:S(2)}) collective-permute-start(f32[1,163840]{1,0:T(1,128)} %get-tuple-element.213), channel_id=1, source_target_pairs={{0,32},{32,64},{64,96},{96,128},{128,160},{160,192},{192,224},{224... | collective-permute-start | bytes 1966088 | tf_op jit(solution)/shard_map/while/body/eval_jaxpr/ppermute | solution.py:14
  576.6 15.5 %collective-permute-done = f32[1,163840]{1,0:T(1,128)S(1)} collective-permute-done((f32[1,163840]{1,0:T(1,128)}, f32[1,163840]{1,0:T(1,128)S(1)}, u32[]{:S(2)}, u32[]{:S(2)}) %collective-permute-start) | collective-permute-done | bytes 655392 | tf_op jit(solution)/shard_map/while/body/eval_jaxpr/ppermute | solution.py:14
  593.7 7.5 %fusion.10 = f32[1,5,8,32,128]{4,1,0,3,2:T(8,128)S(1)} fusion(f32[1,5,8,32,128]{4,1,0,3,2:T(8,128)} %pad_subtract_fusion, f32[1,5,8,32,128]{4,1,0,3,2:T(8,128)} %fusion.12, f32[1,5,8,32,128]{4,1,0,3,2:T(8,128)} %fusion.13, f32[1,5,8,32,128]{4,3,2,1,0:T(8,128)} %param.10, f32[1,5,8,32,128]{4,3,2,1,0:T(8,128)S(1)} %bitcast.56, ...), kind=kOutput, calls=%fused_computation.12 | convolution fusion | flops 33587200 | bytes 7625004 | tf_op jit(solution)/shard_map/dab,dnbijk->naijk/dot_general | solution.py:65
  (79 shorter events, 49.9 us)
Async XLA Ops:
  0.0 593.7 %copy-start = (f32[3,5,5]{2,0,1:T(4,128)S(1)}, f32[3,5,5]{2,0,1:T(4,128)}, u32[]{:S(2)}) copy-start(f32[3,5,5]{2,0,1:T(4,128)} %param.13) | copy-start | bytes 904
  1.1 22.5 %copy-start.3 = (f32[1,5,8,32,128]{4,3,2,1,0:T(8,128)}, f32[1,5,8,32,128]{4,3,2,1,0:T(8,128)S(1)}, u32[]{:S(2)}) copy-start(f32[1,5,8,32,128]{4,3,2,1,0:T(8,128)S(1)} %copy.87) | copy-start | bytes 1966084
  2.1 37.6 %all-to-all-start = ((f32[16,1,2,5,8,128]{5,4,3,2,1,0:T(8,128)}), f32[16,1,2,5,8,128]{5,4,3,2,1,0:T(8,128)S(1)}, u32[]{:S(2)}, u32[]{:S(2)}) async-start(f32[16,1,2,5,8,128]{5,4,3,2,1,0:T(8,128)} %stack.16), calls=%async_computation | async-start | bytes 1310720 | tf_op jit(solution)/shard_map/all_to_all | solution.py:101
  16.0 6.7 %copy-start.7 = (s32[1,2,8,128]{3,2,1,0:T(8,128)S(1)}, s32[1,2,8,128]{3,2,1,0:T(8,128)}, u32[]{:S(2)}) copy-start(s32[1,2,8,128]{3,2,1,0:T(8,128)} %param.15) | copy-start | bytes 24580
  16.0 6.9 %copy-start.6 = (f32[8,32,128]{2,1,0:T(8,128)S(1)}, f32[8,32,128]{2,1,0:T(8,128)}, u32[]{:S(2)}) copy-start(f32[8,32,128]{2,1,0:T(8,128)} %param.11) | copy-start | bytes 393220
  17.2 15.8 %collective-permute-start.2 = (f32[1,5,1,32,128]{4,1,0,3,2:T(8,128)}, f32[1,5,1,32,128]{4,1,0,3,2:T(8,128)S(1)}, u32[]{:S(2)}, u32[]{:S(2)}) collective-permute-start(f32[1,5,1,32,128]{4,1,0,3,2:T(8,128)} %get-tuple-element.150), channel_id=1, source_target_pairs={{0,1},{1,2},{2,3},{3,4},{4,5},{5,6},{6,7},{7,8},{8,9},{9,10},{10,1... | collective-permute-start | bytes 245768 | tf_op jit(solution)/shard_map/ppermute | solution.py:22
  19.1 18.6 %collective-permute-start.1 = (f32[1,5,1,32,128]{4,1,0,3,2:T(8,128)}, f32[1,5,1,32,128]{4,1,0,3,2:T(8,128)}, u32[]{:S(2)}, u32[]{:S(2)}) collective-permute-start(f32[1,5,1,32,128]{4,1,0,3,2:T(8,128)} %get-tuple-element.151), channel_id=1, source_target_pairs={{1,0},{2,1},{3,2},{4,3},{5,4},{6,5},{7,6},{8,7},{9,8},{10,9},{11,1... | collective-permute-start | bytes 245768 | tf_op jit(solution)/shard_map/ppermute | solution.py:25
  25.5 1.4 copy-start.1
  39.7 2.6 copy-start.2
  42.2 2.4 copy-start.4
  42.3 2.4 copy-start.5
  44.7 36.6 %collective-permute-start = (f32[1,163840]{1,0:T(1,128)}, f32[1,163840]{1,0:T(1,128)S(1)}, u32[]{:S(2)}, u32[]{:S(2)}) collective-permute-start(f32[1,163840]{1,0:T(1,128)} %get-tuple-element.213), channel_id=1, source_target_pairs={{0,32},{32,64},{64,96},{96,128},{128,160},{160,192},{192,224},{224... | collective-permute-start | bytes 1966088 | tf_op jit(solution)/shard_map/while/body/eval_jaxpr/ppermute | solution.py:14
  82.9 18.1 %collective-permute-start = (f32[1,163840]{1,0:T(1,128)}, f32[1,163840]{1,0:T(1,128)S(1)}, u32[]{:S(2)}, u32[]{:S(2)}) collective-permute-start(f32[1,163840]{1,0:T(1,128)} %get-tuple-element.213), channel_id=1, source_target_pairs={{0,32},{32,64},{64,96},{96,128},{128,160},{160,192},{192,224},{224... | collective-permute-start | bytes 1966088 | tf_op jit(solution)/shard_map/while/body/eval_jaxpr/ppermute | solution.py:14
  102.6 25.5 %collective-permute-start = (f32[1,163840]{1,0:T(1,128)}, f32[1,163840]{1,0:T(1,128)S(1)}, u32[]{:S(2)}, u32[]{:S(2)}) collective-permute-start(f32[1,163840]{1,0:T(1,128)} %get-tuple-element.213), channel_id=1, source_target_pairs={{0,32},{32,64},{64,96},{96,128},{128,160},{160,192},{192,224},{224... | collective-permute-start | bytes 1966088 | tf_op jit(solution)/shard_map/while/body/eval_jaxpr/ppermute | solution.py:14
  129.7 52.3 %collective-permute-start = (f32[1,163840]{1,0:T(1,128)}, f32[1,163840]{1,0:T(1,128)S(1)}, u32[]{:S(2)}, u32[]{:S(2)}) collective-permute-start(f32[1,163840]{1,0:T(1,128)} %get-tuple-element.213), channel_id=1, source_target_pairs={{0,32},{32,64},{64,96},{96,128},{128,160},{160,192},{192,224},{224... | collective-permute-start | bytes 1966088 | tf_op jit(solution)/shard_map/while/body/eval_jaxpr/ppermute | solution.py:14
  183.6 52.9 %collective-permute-start = (f32[1,163840]{1,0:T(1,128)}, f32[1,163840]{1,0:T(1,128)S(1)}, u32[]{:S(2)}, u32[]{:S(2)}) collective-permute-start(f32[1,163840]{1,0:T(1,128)} %get-tuple-element.213), channel_id=1, source_target_pairs={{0,32},{32,64},{64,96},{96,128},{128,160},{160,192},{192,224},{224... | collective-permute-start | bytes 1966088 | tf_op jit(solution)/shard_map/while/body/eval_jaxpr/ppermute | solution.py:14
  238.1 33.8 %collective-permute-start = (f32[1,163840]{1,0:T(1,128)}, f32[1,163840]{1,0:T(1,128)S(1)}, u32[]{:S(2)}, u32[]{:S(2)}) collective-permute-start(f32[1,163840]{1,0:T(1,128)} %get-tuple-element.213), channel_id=1, source_target_pairs={{0,32},{32,64},{64,96},{96,128},{128,160},{160,192},{192,224},{224... | collective-permute-start | bytes 1966088 | tf_op jit(solution)/shard_map/while/body/eval_jaxpr/ppermute | solution.py:14
  273.5 60.9 %collective-permute-start = (f32[1,163840]{1,0:T(1,128)}, f32[1,163840]{1,0:T(1,128)S(1)}, u32[]{:S(2)}, u32[]{:S(2)}) collective-permute-start(f32[1,163840]{1,0:T(1,128)} %get-tuple-element.213), channel_id=1, source_target_pairs={{0,32},{32,64},{64,96},{96,128},{128,160},{160,192},{192,224},{224... | collective-permute-start | bytes 1966088 | tf_op jit(solution)/shard_map/while/body/eval_jaxpr/ppermute | solution.py:14
  336.0 34.2 %collective-permute-start = (f32[1,163840]{1,0:T(1,128)}, f32[1,163840]{1,0:T(1,128)S(1)}, u32[]{:S(2)}, u32[]{:S(2)}) collective-permute-start(f32[1,163840]{1,0:T(1,128)} %get-tuple-element.213), channel_id=1, source_target_pairs={{0,32},{32,64},{64,96},{96,128},{128,160},{160,192},{192,224},{224... | collective-permute-start | bytes 1966088 | tf_op jit(solution)/shard_map/while/body/eval_jaxpr/ppermute | solution.py:14
  371.8 31.6 %collective-permute-start = (f32[1,163840]{1,0:T(1,128)}, f32[1,163840]{1,0:T(1,128)S(1)}, u32[]{:S(2)}, u32[]{:S(2)}) collective-permute-start(f32[1,163840]{1,0:T(1,128)} %get-tuple-element.213), channel_id=1, source_target_pairs={{0,32},{32,64},{64,96},{96,128},{128,160},{160,192},{192,224},{224... | collective-permute-start | bytes 1966088 | tf_op jit(solution)/shard_map/while/body/eval_jaxpr/ppermute | solution.py:14
  405.0 44.9 %collective-permute-start = (f32[1,163840]{1,0:T(1,128)}, f32[1,163840]{1,0:T(1,128)S(1)}, u32[]{:S(2)}, u32[]{:S(2)}) collective-permute-start(f32[1,163840]{1,0:T(1,128)} %get-tuple-element.213), channel_id=1, source_target_pairs={{0,32},{32,64},{64,96},{96,128},{128,160},{160,192},{192,224},{224... | collective-permute-start | bytes 1966088 | tf_op jit(solution)/shard_map/while/body/eval_jaxpr/ppermute | solution.py:14
  451.6 31.7 %collective-permute-start = (f32[1,163840]{1,0:T(1,128)}, f32[1,163840]{1,0:T(1,128)S(1)}, u32[]{:S(2)}, u32[]{:S(2)}) collective-permute-start(f32[1,163840]{1,0:T(1,128)} %get-tuple-element.213), channel_id=1, source_target_pairs={{0,32},{32,64},{64,96},{96,128},{128,160},{160,192},{192,224},{224... | collective-permute-start | bytes 1966088 | tf_op jit(solution)/shard_map/while/body/eval_jaxpr/ppermute | solution.py:14
  484.9 35.0 %collective-permute-start = (f32[1,163840]{1,0:T(1,128)}, f32[1,163840]{1,0:T(1,128)S(1)}, u32[]{:S(2)}, u32[]{:S(2)}) collective-permute-start(f32[1,163840]{1,0:T(1,128)} %get-tuple-element.213), channel_id=1, source_target_pairs={{0,32},{32,64},{64,96},{96,128},{128,160},{160,192},{192,224},{224... | collective-permute-start | bytes 1966088 | tf_op jit(solution)/shard_map/while/body/eval_jaxpr/ppermute | solution.py:14
  521.5 21.9 %collective-permute-start = (f32[1,163840]{1,0:T(1,128)}, f32[1,163840]{1,0:T(1,128)S(1)}, u32[]{:S(2)}, u32[]{:S(2)}) collective-permute-start(f32[1,163840]{1,0:T(1,128)} %get-tuple-element.213), channel_id=1, source_target_pairs={{0,32},{32,64},{64,96},{96,128},{128,160},{160,192},{192,224},{224... | collective-permute-start | bytes 1966088 | tf_op jit(solution)/shard_map/while/body/eval_jaxpr/ppermute | solution.py:14
  545.0 23.2 %collective-permute-start = (f32[1,163840]{1,0:T(1,128)}, f32[1,163840]{1,0:T(1,128)S(1)}, u32[]{:S(2)}, u32[]{:S(2)}) collective-permute-start(f32[1,163840]{1,0:T(1,128)} %get-tuple-element.213), channel_id=1, source_target_pairs={{0,32},{32,64},{64,96},{96,128},{128,160},{160,192},{192,224},{224... | collective-permute-start | bytes 1966088 | tf_op jit(solution)/shard_map/while/body/eval_jaxpr/ppermute | solution.py:14
  569.8 22.3 %collective-permute-start = (f32[1,163840]{1,0:T(1,128)}, f32[1,163840]{1,0:T(1,128)S(1)}, u32[]{:S(2)}, u32[]{:S(2)}) collective-permute-start(f32[1,163840]{1,0:T(1,128)} %get-tuple-element.213), channel_id=1, source_target_pairs={{0,32},{32,64},{64,96},{96,128},{128,160},{160,192},{192,224},{224... | collective-permute-start | bytes 1966088 | tf_op jit(solution)/shard_map/while/body/eval_jaxpr/ppermute | solution.py:14
